TPU v7x, 256 devices: a whole 4x4x8 slice. The times are simulated.
256 devices in a mesh: tok: 32 (over x, z), hid: 8 (over y, core).
Axes of the slice: x: 4, y: 4, z: 8, core: 2. Of those that a mesh axis runs over, the one named last changes fastest.
Arguments:
- tokens: bfloat16 [16384, 5376], P('tok', 'hid'), may hold values from -6 to 6
- norm_gain: bfloat16 [1, 5376], P(None, 'hid'), may hold values from 0.099609375 to 1.8984375
- w_query: bfloat16 [5376, 4096], P('tok', 'hid'), may hold values from -2 to 2
- w_key: bfloat16 [5376, 2048], P('tok', 'hid'), may hold values from -1 to 1
- value_matrix: bfloat16 [5376, 2048], P('tok', 'hid'), may hold values from -0.078125 to 0.078125
- q_norm_gain: bfloat16 [1, 128], replicated, may hold values from 0.1 to 8
- k_norm_gain: bfloat16 [1, 128], replicated, may hold values from 0.1 to 8
- w_out: bfloat16 [4096, 5376], P('hid'), may hold values from -0.125 to 0.125
Outputs:
- attended: bfloat16 [16384, 5376], P('tok', 'hid')
All inputs are finite; a program needn't handle non-finite values.
Results may differ from a plain program's by a relative error of at most 0.017.
Values may be sent and summed in bfloat16 or wider, within the bound.
No kernel may reach another device: no remote copies, remote signals or barrier semaphores. Data moves between devices by JAX's collectives and lax.ppermute only.
A program may use at most 64 MiB of HBM per device.

v0:
```python
import math
import jax
import jax.numpy as jnp
from jax import lax
from jax.sharding import PartitionSpec as P

HEAD_SIZE = 128
WINDOW = 1024
TOK = ("tx", "tz")
HID = ("hy", "hc")
score_scale = 168.0 ** (-0.5)


def shifted(value, axis, steps):
    count = lax.axis_size(axis)
    leading, last = (max(0, -steps), min(count, count - steps))
    return lax.ppermute(value, axis, [(source, source + steps) for source in range(leading, last)])


def head_norm(field, gain):
    count = field.shape[0]
    heads = field.reshape(count, -1, HEAD_SIZE)
    mean_square = jnp.mean(heads * heads, axis=-1, keepdims=True)
    scaled = (
        heads * lax.rsqrt(mean_square + 1e-06) * gain.astype(jnp.float32).reshape(1, 1, HEAD_SIZE)
    )
    return scaled.reshape(count, -1)


def rotate(field, positions):
    count = field.shape[0]
    heads = field.reshape(count, -1, HEAD_SIZE)
    half = HEAD_SIZE // 2
    inverse = jnp.exp(-math.log(10000.0) * jnp.arange(half, dtype=jnp.float32) * 2.0 / HEAD_SIZE)
    angles = positions.astype(jnp.float32)[:, None] * inverse[None, :]
    cosine = jnp.cos(angles)[:, None, :]
    sine = jnp.sin(angles)[:, None, :]
    first = heads[..., :half]
    second = heads[..., half:]
    turned = jnp.concatenate(
        [first * cosine - second * sine, second * cosine + first * sine], axis=-1
    )
    return turned.reshape(count, -1)


def local(tokens, norm_gain, w_query, w_key, value_matrix, q_norm_gain, k_norm_gain, w_out):
    rows = tokens.shape[0]
    with_gain = jnp.concatenate([tokens, norm_gain], axis=0)
    n_hid = lax.axis_size(HID)
    hid_index = lax.axis_index(HID)
    received = [with_gain] + [
        lax.ppermute(with_gain, HID, [(i, (i + k) % n_hid) for i in range(n_hid)])
        for k in range(1, n_hid)
    ]
    by_shift = jnp.stack(received)
    ordered = jnp.take(by_shift, (hid_index - jnp.arange(n_hid)) % n_hid, axis=0)
    values32 = ordered[:, :rows].astype(jnp.float32)
    gain_rows = ordered[:, rows:].astype(jnp.float32)
    mean_square = jnp.sum(values32 * values32, axis=(0, 2)) / (n_hid * values32.shape[2])
    scale_rows = lax.rsqrt(mean_square + 1e-06)[None, :, None]
    normed = (values32 * scale_rows * gain_rows).astype(jnp.bfloat16)
    width_query = w_query.shape[1]
    width_kv = w_key.shape[1]
    stacked = lax.all_gather(
        lax.all_gather(
            jnp.concatenate([w_query, w_key, value_matrix], axis=1), "tz", axis=0, tiled=True
        ),
        "tx",
        axis=0,
        tiled=True,
    )
    weights3 = stacked.reshape(n_hid, normed.shape[2], stacked.shape[1])
    projected_kv = jnp.einsum(
        "jrc,jcn->rn", normed, weights3[:, :, width_query:], preferred_element_type=jnp.float32
    )
    key_raw = projected_kv[:, :width_kv]
    value_raw = projected_kv[:, width_kv:]
    tok_index = lax.axis_index(TOK)
    positions = tok_index * rows + jnp.arange(rows, dtype=jnp.int32)
    key = rotate(head_norm(key_raw, k_norm_gain), positions).astype(jnp.bfloat16)
    value_rows = value_raw.astype(jnp.bfloat16)
    joined = jnp.concatenate([key, value_rows], axis=1)
    reach = (WINDOW - 1 + rows - 1) // rows
    earlier = [shifted(joined, TOK, offset) for offset in range(reach, 0, -1)]
    normed_late, _ = lax.optimization_barrier((normed, joined))
    query_raw = jnp.einsum(
        "jrc,jcn->rn", normed_late, weights3[:, :, :width_query], preferred_element_type=jnp.float32
    )
    query = rotate(head_norm(query_raw, q_norm_gain), positions).astype(jnp.bfloat16)
    window_kv = jnp.concatenate(earlier + [joined], axis=0)
    window_extent = window_kv.shape[0]
    key_pos = (tok_index - reach) * rows + jnp.arange(window_extent, dtype=jnp.int32)
    kv_heads = width_kv // HEAD_SIZE
    query_group_count = width_query // HEAD_SIZE // kv_heads
    query_four_axes = query.reshape(rows, kv_heads, query_group_count, HEAD_SIZE)
    keys_three_axes = window_kv[:, :width_kv].reshape(window_extent, kv_heads, HEAD_SIZE)
    values_three_axes = window_kv[:, width_kv:].reshape(window_extent, kv_heads, HEAD_SIZE)
    scores = (
        jnp.einsum(
            "tkgd,skd->kgts", query_four_axes, keys_three_axes, preferred_element_type=jnp.float32
        )
        * score_scale
    )
    allowed = (
        (key_pos[None, :] <= positions[:, None])
        & (key_pos[None, :] > positions[:, None] - WINDOW)
        & (key_pos[None, :] >= 0)
    )
    masked = jnp.where(allowed, scores, -1e30)
    top = jnp.max(masked, axis=-1, keepdims=True)
    weights = jnp.where(allowed, jnp.exp(masked - top), 0.0)
    total = jnp.sum(weights, axis=-1)
    probs = weights.astype(jnp.bfloat16)
    mixed = jnp.einsum(
        "kgts,skd->tkgd", probs, values_three_axes, preferred_element_type=jnp.float32
    )
    mixed = mixed / jnp.transpose(total, (2, 0, 1))[..., None]
    heads_out = mixed.reshape(rows, width_query).astype(jnp.bfloat16)
    partial_value = jnp.dot(heads_out, w_out, preferred_element_type=jnp.float32)
    return lax.psum_scatter(
        partial_value.astype(jnp.bfloat16), HID, scatter_dimension=1, tiled=True
    )


def solution(mesh):
    devices = mesh.devices
    n_x = len({d.coords[0] for d in devices.flat})
    n_y = len({d.coords[1] for d in devices.flat})
    split = jax.sharding.Mesh(
        devices.reshape(n_x, devices.shape[0] // n_x, n_y, devices.shape[1] // n_y),
        ("tx", "tz", "hy", "hc"),
    )
    in_specs = (
        P(TOK, HID),
        P(None, HID),
        P(TOK, HID),
        P(TOK, HID),
        P(TOK, HID),
        P(),
        P(),
        P(HID, None),
    )
    out_specs = P(TOK, HID)
    return jax.shard_map(local, mesh=split, in_specs=in_specs, out_specs=out_specs, check_vma=False)
```

profile of v0, /device:TPU:2, one launch (start us, length us, event | category | flops | bytes accessed | tf_op | source)
XLA Modules:
  0.0 282.9 jit_solution(6416758314910907047)
XLA Ops:
  6.5 0.0 copy-start.2
  6.5 0.0 all-gather.3.cloned.1.call-start
  6.5 1.8 pad_maximum_fusion.3
  8.4 0.0 all-gather.3.cloned.1.call-update
  8.4 0.0 all-gather.5.cloned.1.call-start
  8.4 46.3 %all-gather.3.cloned.1.call-done = bf16[1344,1024]{1,0:T(8,128)(2,1)} async-done(((bf16[168,1024]{1,0:T(8,128)(2,1)}), bf16[1344,1024]{1,0:T(8,128)(2,1)}) %all-gather.3.cloned.1.call-update) | async-done | bytes 2752528 | tf_op jit(solution)/shard_map/all_gather | solution.py:65
  54.8 0.0 all-gather.5.cloned.1.call-update
  54.8 0.0 reduce-scatter.2.cloned.1.call-start
  54.8 1.4 copy.19
  56.2 0.8 pad_maximum_fusion
  57.0 0.0 collective-permute-start
  57.0 1.6 collective-permute-start.1
  58.6 2.0 collective-permute-start.2
  60.6 2.0 collective-permute-start.3
  62.6 1.6 collective-permute-start.4
  64.3 0.5 multiply_cosine_fusion
  64.9 1.9 and_and_fusion
  66.8 0.0 copy-done.3
  66.8 0.0 copy-done.4
  66.8 0.0 copy-done.2
  66.8 1.0 bitcast_dynamic-update-slice_fusion.7
  67.8 9.9 %collective-permute-done = bf16[513,672]{1,0:T(8,128)(2,1)} collective-permute-done((bf16[513,672]{1,0:T(8,128)(2,1)S(1)}, bf16[513,672]{1,0:T(8,128)(2,1)}, u32[]{:S(2)}, u32[]{:S(2)}) %collective-permute-start) | collective-permute-done | bytes 689504 | tf_op jit(solution)/shard_map/ppermute | solution.py:52
  77.7 1.5 collective-permute-start.5
  79.3 2.1 bitcast_dynamic-update-slice_fusion.6
  81.4 0.0 collective-permute-done.1
  81.4 14.7 %collective-permute-start.6 = (bf16[513,672]{1,0:T(8,128)(2,1)S(1)}, bf16[513,672]{1,0:T(8,128)(2,1)S(1)}, u32[]{:S(2)}, u32[]{:S(2)}) collective-permute-start(bf16[513,672]{1,0:T(8,128)(2,1)S(1)} %pad_maximum_fusion), channel_id=1, source_target_pairs={{0,7},{1,0},{2,1},{3,2},{4,3},{5,4},{6,5},{7,6},{8,15},{9,8},{10,9... | collective-permute-start | bytes 2068424 | tf_op jit(solution)/shard_map/ppermute | solution.py:52
  96.1 2.1 bitcast_dynamic-update-slice_fusion.5
  98.2 14.7 %collective-permute-done.2 = bf16[513,672]{1,0:T(8,128)(2,1)} collective-permute-done((bf16[513,672]{1,0:T(8,128)(2,1)S(1)}, bf16[513,672]{1,0:T(8,128)(2,1)}, u32[]{:S(2)}, u32[]{:S(2)}) %collective-permute-start.2) | collective-permute-done | bytes 689504 | tf_op jit(solution)/shard_map/ppermute | solution.py:52
  112.9 2.1 bitcast_dynamic-update-slice_fusion.4
  115.0 0.0 collective-permute-done.3
  115.0 1.0 bitcast_dynamic-update-slice_fusion.3
  116.0 11.4 %collective-permute-done.4 = bf16[513,672]{1,0:T(8,128)(2,1)S(1)} collective-permute-done((bf16[513,672]{1,0:T(8,128)(2,1)S(1)}, bf16[513,672]{1,0:T(8,128)(2,1)S(1)}, u32[]{:S(2)}, u32[]{:S(2)}) %collective-permute-start.4) | collective-permute-done | bytes 689504 | tf_op jit(solution)/shard_map/ppermute | solution.py:52
  127.4 1.0 bitcast_dynamic-update-slice_fusion.2
  128.4 0.0 collective-permute-done.5
  128.4 1.0 bitcast_dynamic-update-slice_fusion.1
  129.4 0.2 collective-permute-done.6
  129.6 0.9 bitcast_dynamic-update-slice_fusion
  130.5 6.5 %gather_fusion = bf16[8,513,672]{2,1,0:T(8,128)(2,1)} fusion(bf16[8,513,672]{2,1,0:T(8,128)(2,1)} %bitcast_dynamic-update-slice_fusion, s32[1024]{0:T(1024)S(1)} %pad_clamp_fusion), kind=kCustom, calls=%fused_computation | custom fusion | bytes 11031584 | tf_op jit(solution)/shard_map/jit(_take)/gather | solution.py:56
  137.0 3.5 %broadcast_select_fusion = bf16[8,513,672]{2,1,0:T(8,128)(2,1)S(1)} fusion(bf16[8,513,672]{2,1,0:T(8,128)(2,1)} %gather_fusion, pred[8]{0:T(512)(128)(4,1)S(1)} %compare_and_fusion), kind=kLoop, calls=%fused_computation.11 | loop fusion | flops 2757888 | bytes 11031560 | tf_op jit(solution)/shard_map/jit(_take)/select_n | solution.py:56
  140.6 1.4 fusion.1
  142.0 4.7 %fusion.3 = bf16[8,512,672]{2,1,0:T(8,128)(2,1)} fusion(f32[8,672]{1,0:T(8,128)S(1)} %bitcast.85, f32[512]{0:T(512)S(1)} %add_rsqrt_fusion.2, bf16[8,513,672]{2,1,0:T(8,128)(2,1)S(1)} %broadcast_select_fusion), kind=kLoop, calls=%fused_computation.6 | loop fusion | flops 11010048 | bytes 11033600 | tf_op jit(solution)/shard_map/convert_element_type | solution.py:61
  146.6 16.5 %all-gather.5.cloned.1.call-done = bf16[5376,1024]{1,0:T(8,128)(2,1)} async-done(((bf16[1344,1024]{1,0:T(8,128)(2,1)}), bf16[5376,1024]{1,0:T(8,128)(2,1)}) %all-gather.5.cloned.1.call-update) | async-done | bytes 11010064 | tf_op jit(solution)/shard_map/all_gather | solution.py:64
  163.1 8.3 %fusion.14 = f32[512,512]{0,1:T(8,128)S(1)} fusion(bf16[8,512,672]{2,1,0:T(8,128)(2,1)} %fusion.3, bf16[8,672,1024]{2,1,0:T(8,128)(2,1)} %bitcast.86), kind=kOutput, calls=%fused_computation.23 | convolution fusion | flops 2818572288 | bytes 12845056 | tf_op jit(solution)/shard_map/jrc,jcn->rn/dot_general | solution.py:73
  171.4 0.1 multiply_reduce_fusion.1
  171.6 0.1 multiply_multiply_fusion.1
  171.7 0.1 subtract_convert_fusion.1
  171.8 4.5 %collective-permute-start.7 = (bf16[512,512]{0,1:T(8,128)(2,1)S(1)}, bf16[512,512]{0,1:T(8,128)(2,1)S(1)}, u32[]{:S(2)}, u32[]{:S(2)}) collective-permute-start(bf16[512,512]{0,1:T(8,128)(2,1)S(1)} %pad_maximum_fusion.1), channel_id=1, source_target_pairs={{0,16},{8,24},{16,32},{24,40},{32,48},{40,56},{48,64},{56,72},{64,... | collective-permute-start | bytes 1572872 | tf_op jit(solution)/shard_map/ppermute | solution.py:17
  176.3 3.7 %collective-permute-start.8 = (bf16[512,512]{0,1:T(8,128)(2,1)S(1)}, bf16[512,512]{0,1:T(8,128)(2,1)S(1)}, u32[]{:S(2)}, u32[]{:S(2)}) collective-permute-start(bf16[512,512]{0,1:T(8,128)(2,1)S(1)} %pad_maximum_fusion.1), channel_id=1, source_target_pairs={{0,8},{8,16},{16,24},{24,32},{32,40},{40,48},{48,56},{56,64},{64,7... | collective-permute-start | bytes 1572872 | tf_op jit(solution)/shard_map/ppermute | solution.py:17
  180.0 0.0 copy-done
  180.0 5.5 %fusion.10 = f32[512,512,1]{0,1,2:T(8,128)S(1)} fusion(bf16[8,512,672]{2,1,0:T(8,128)(2,1)S(1)} %copy-done, bf16[8,672,1024]{2,1,0:T(8,128)(2,1)} %bitcast.87), kind=kOutput, calls=%fused_computation.17 | convolution fusion | flops 2818572288 | bytes 12058624 | tf_op jit(solution)/shard_map/jrc,jcn->rn/dot_general | solution.py:86
  185.5 0.0 copy-start.1
  185.6 0.1 multiply_reduce_fusion
  185.7 0.2 multiply_multiply_fusion
  185.9 0.2 subtract_convert_fusion
  186.1 15.8 %collective-permute-done.7 = bf16[512,512]{0,1:T(8,128)(2,1)S(1)} collective-permute-done((bf16[512,512]{0,1:T(8,128)(2,1)S(1)}, bf16[512,512]{0,1:T(8,128)(2,1)S(1)}, u32[]{:S(2)}, u32[]{:S(2)}) %collective-permute-start.7) | collective-permute-done | bytes 524320 | tf_op jit(solution)/shard_map/ppermute | solution.py:17
  201.9 10.8 %collective-permute-done.8 = bf16[512,512]{0,1:T(8,128)(2,1)S(1)} collective-permute-done((bf16[512,512]{0,1:T(8,128)(2,1)S(1)}, bf16[512,512]{0,1:T(8,128)(2,1)S(1)}, u32[]{:S(2)}, u32[]{:S(2)}) %collective-permute-start.8) | collective-permute-done | bytes 524320 | tf_op jit(solution)/shard_map/ppermute | solution.py:17
  212.7 0.1 maximum_maximum_fusion
  212.8 0.1 fusion.35
  212.9 0.0 copy-done.1
  212.9 8.5 %fusion.36 = (f32[2,2,512]{2,1,0:T(2,128)S(1)}, bf16[2,2,512,1536]{2,3,1,0:T(8,128)(2,1)}) fusion(pred[512,1536]{0,1:T(8,128)(4,1)S(1)} %copy-done.1, bf16[1536,2,128,1]{0,2,3,1:T(8,128)(2,1)S(1)} %bitcast.83, bf16[512,2,2,128]{0,3,2,1:T(8,128)(2,1)S(1)} %bitcast.84), kind=kOutput, calls=%fused_computation.81 | convolution fusion | flops 824182272 | bytes 8396800 | tf_op jit(solution)/shard_map/sub | solution.py:111
  221.4 3.8 %fusion.25 = bf16[512,2,2,128]{0,3,2,1:T(8,128)(2,1)S(1)} fusion(bf16[1536,2,128,1]{0,2,3,1:T(8,128)(2,1)S(1)} %bitcast.82, bf16[2,2,512,1536]{2,3,1,0:T(8,128)(2,1)} %get-tuple-element.16, f32[512,2,2]{0,2,1:T(2,128)S(1)} %bitcast.89), kind=kOutput, calls=%fused_computation.27 | convolution fusion | flops 805830656 | bytes 7610368 | tf_op jit(solution)/shard_map/kgts,skd->tkgd/dot_general | solution.py:114
  225.2 8.6 %convolution_convert_fusion = bf16[512,5376]{0,1:T(8,128)(2,1)} fusion(bf16[512,512]{0,1:T(8,128)(2,1)S(1)} %bitcast.88, bf16[512,5376]{1,0:T(8,128)(2,1)} %param.15), kind=kOutput, calls=%fused_computation.10 | convolution fusion | flops 2821324800 | bytes 11534336 | tf_op jit(solution)/shard_map/dot_general | solution.py:119
  233.8 0.0 reduce-scatter.2.cloned.1.call-update
  233.9 42.5 %reduce-scatter.2.cloned.1.call-done = bf16[512,672]{0,1:T(8,128)(2,1)} async-done(((bf16[512,5376]{0,1:T(8,128)(2,1)}), bf16[512,672]{0,1:T(8,128)(2,1)}) %reduce-scatter.2.cloned.1.call-update) | async-done | bytes 688144 | tf_op jit(solution)/shard_map/reduce_scatter | solution.py:120
  (22 shorter events, 0.3 us)
Async XLA Ops:
  6.5 60.3 %copy-start.2 = (bf16[1,672]{1,0:T(2,128)(2,1)S(1)}, bf16[1,672]{1,0:T(2,128)(2,1)}, u32[]{:S(2)}) copy-start(bf16[1,672]{1,0:T(2,128)(2,1)} %param.9) | copy-start | bytes 4036
  6.5 60.3 %copy-start.3 = (bf16[1,128]{1,0:T(2,128)(2,1)S(1)}, bf16[1,128]{1,0:T(2,128)(2,1)}, u32[]{:S(2)}) copy-start(bf16[1,128]{1,0:T(2,128)(2,1)} %param.14) | copy-start | bytes 772
  6.5 60.3 %copy-start.4 = (bf16[1,128]{1,0:T(2,128)(2,1)S(1)}, bf16[1,128]{1,0:T(2,128)(2,1)}, u32[]{:S(2)}) copy-start(bf16[1,128]{1,0:T(2,128)(2,1)} %param.13) | copy-start | bytes 772
  6.5 48.2 %all-gather.3.cloned.1.call-start = ((), (), s32[]{:S(2)}) async-start(), calls=%async_computation.1 | async-start | bytes 3096576 | tf_op jit(solution)/shard_map/all_gather | solution.py:65
  8.4 154.7 %all-gather.5.cloned.1.call-start = ((), (), s32[]{:S(2)}) async-start(), calls=%async_computation.2 | async-start | bytes 13762560 | tf_op jit(solution)/shard_map/all_gather | solution.py:64
  54.8 221.6 %reduce-scatter.2.cloned.1.call-start = ((), (), s32[]{:S(2)}) async-start(), calls=%async_computation.3 | async-start | bytes 6193152 | tf_op jit(solution)/shard_map/reduce_scatter | solution.py:120
  57.0 20.8 %collective-permute-start = (bf16[513,672]{1,0:T(8,128)(2,1)S(1)}, bf16[513,672]{1,0:T(8,128)(2,1)}, u32[]{:S(2)}, u32[]{:S(2)}) collective-permute-start(bf16[513,672]{1,0:T(8,128)(2,1)S(1)} %pad_maximum_fusion), channel_id=1, source_target_pairs={{0,1},{1,2},{2,3},{3,4},{4,5},{5,6},{6,7},{7,0},{8,9},{9,10},{10,1... | collective-permute-start | bytes 2068424 | tf_op jit(solution)/shard_map/ppermute | solution.py:52
  57.0 24.4 %collective-permute-start.1 = (bf16[513,672]{1,0:T(8,128)(2,1)S(1)}, bf16[513,672]{1,0:T(8,128)(2,1)}, u32[]{:S(2)}, u32[]{:S(2)}) collective-permute-start(bf16[513,672]{1,0:T(8,128)(2,1)S(1)} %pad_maximum_fusion), channel_id=1, source_target_pairs={{0,2},{1,3},{2,4},{3,5},{4,6},{5,7},{6,0},{7,1},{8,10},{9,11},{10,... | collective-permute-start | bytes 2068424 | tf_op jit(solution)/shard_map/ppermute | solution.py:52
  58.6 54.4 %collective-permute-start.2 = (bf16[513,672]{1,0:T(8,128)(2,1)S(1)}, bf16[513,672]{1,0:T(8,128)(2,1)}, u32[]{:S(2)}, u32[]{:S(2)}) collective-permute-start(bf16[513,672]{1,0:T(8,128)(2,1)S(1)} %pad_maximum_fusion), channel_id=1, source_target_pairs={{0,3},{1,4},{2,5},{3,6},{4,7},{5,0},{6,1},{7,2},{8,11},{9,12},{10,... | collective-permute-start | bytes 2068424 | tf_op jit(solution)/shard_map/ppermute | solution.py:52
  60.6 54.4 %collective-permute-start.3 = (bf16[513,672]{1,0:T(8,128)(2,1)S(1)}, bf16[513,672]{1,0:T(8,128)(2,1)S(1)}, u32[]{:S(2)}, u32[]{:S(2)}) collective-permute-start(bf16[513,672]{1,0:T(8,128)(2,1)S(1)} %pad_maximum_fusion), channel_id=1, source_target_pairs={{0,4},{1,5},{2,6},{3,7},{4,0},{5,1},{6,2},{7,3},{8,12},{9,13},{10,... | collective-permute-start | bytes 2068424 | tf_op jit(solution)/shard_map/ppermute | solution.py:52
  62.6 64.8 %collective-permute-start.4 = (bf16[513,672]{1,0:T(8,128)(2,1)S(1)}, bf16[513,672]{1,0:T(8,128)(2,1)S(1)}, u32[]{:S(2)}, u32[]{:S(2)}) collective-permute-start(bf16[513,672]{1,0:T(8,128)(2,1)S(1)} %pad_maximum_fusion), channel_id=1, source_target_pairs={{0,5},{1,6},{2,7},{3,0},{4,1},{5,2},{6,3},{7,4},{8,13},{9,14},{10,... | collective-permute-start | bytes 2068424 | tf_op jit(solution)/shard_map/ppermute | solution.py:52
  77.7 50.7 %collective-permute-start.5 = (bf16[513,672]{1,0:T(8,128)(2,1)S(1)}, bf16[513,672]{1,0:T(8,128)(2,1)S(1)}, u32[]{:S(2)}, u32[]{:S(2)}) collective-permute-start(bf16[513,672]{1,0:T(8,128)(2,1)S(1)} %pad_maximum_fusion), channel_id=1, source_target_pairs={{0,6},{1,7},{2,0},{3,1},{4,2},{5,3},{6,4},{7,5},{8,14},{9,15},{10,... | collective-permute-start | bytes 2068424 | tf_op jit(solution)/shard_map/ppermute | solution.py:52
  81.4 48.2 %collective-permute-start.6 = (bf16[513,672]{1,0:T(8,128)(2,1)S(1)}, bf16[513,672]{1,0:T(8,128)(2,1)S(1)}, u32[]{:S(2)}, u32[]{:S(2)}) collective-permute-start(bf16[513,672]{1,0:T(8,128)(2,1)S(1)} %pad_maximum_fusion), channel_id=1, source_target_pairs={{0,7},{1,0},{2,1},{3,2},{4,3},{5,4},{6,5},{7,6},{8,15},{9,8},{10,9... | collective-permute-start | bytes 2068424 | tf_op jit(solution)/shard_map/ppermute | solution.py:52
  163.1 16.9 %copy-start = (bf16[8,512,672]{2,1,0:T(8,128)(2,1)S(1)}, bf16[8,512,672]{2,1,0:T(8,128)(2,1)}, u32[]{:S(2)}) copy-start(bf16[8,512,672]{2,1,0:T(8,128)(2,1)} %fusion.3) | copy-start | bytes 16515076
  171.8 30.0 %collective-permute-start.7 = (bf16[512,512]{0,1:T(8,128)(2,1)S(1)}, bf16[512,512]{0,1:T(8,128)(2,1)S(1)}, u32[]{:S(2)}, u32[]{:S(2)}) collective-permute-start(bf16[512,512]{0,1:T(8,128)(2,1)S(1)} %pad_maximum_fusion.1), channel_id=1, source_target_pairs={{0,16},{8,24},{16,32},{24,40},{32,48},{40,56},{48,64},{56,72},{64,... | collective-permute-start | bytes 1572872 | tf_op jit(solution)/shard_map/ppermute | solution.py:17
  176.3 36.4 %collective-permute-start.8 = (bf16[512,512]{0,1:T(8,128)(2,1)S(1)}, bf16[512,512]{0,1:T(8,128)(2,1)S(1)}, u32[]{:S(2)}, u32[]{:S(2)}) collective-permute-start(bf16[512,512]{0,1:T(8,128)(2,1)S(1)} %pad_maximum_fusion.1), channel_id=1, source_target_pairs={{0,8},{8,16},{16,24},{24,32},{32,40},{40,48},{48,56},{56,64},{64,7... | collective-permute-start | bytes 1572872 | tf_op jit(solution)/shard_map/ppermute | solution.py:17
  185.5 27.4 %copy-start.1 = (pred[512,1536]{0,1:T(8,128)(4,1)S(1)}, pred[512,1536]{0,1:T(8,128)(4,1)}, u32[]{:S(2)}) copy-start(pred[512,1536]{0,1:T(8,128)(4,1)} %and_and_fusion) | copy-start | bytes 2359300
Sparse Core Ops, SparseCore 0:
  9.1 45.5 all-gather.2
  56.6 106.4 all-gather.4
  234.0 42.3 reduce-scatter.1
where the time goes:
time: 283 us
  waiting for transfers between devices  168 us (59%)
  matrix products  34.7 us (12%)
  starting transfers between devices  31.7 us (11%)
  local copies, waits for them, and re-layouts  18.2 us (6%)
  other arithmetic  16.6 us (6%)
  between operations  13.4 us (5%)
    all_gather x1, waiting for transfers between devices, local(): lax.all_gather(jnp.concatenate([w_query, w_key, value_matrix], axis=1), '...  46.3 us
    reduce_scatter x1, waiting for transfers between devices, local(): lax.psum_scatter(partial_value.astype(jnp.bfloat16), HID, scatter_dimensi...  42.5 us
    ppermute x7, waiting for transfers between devices, local(): lax.ppermute(with_gain, HID, [(i, (i + k) % n_hid) for i in range(n_hid)])  36.3 us
    ppermute x2, waiting for transfers between devices, shifted(): lax.ppermute(value, axis, [(source, source + steps) for source in range(l...  26.6 us
    ppermute x7, starting transfers between devices, local(): lax.ppermute(with_gain, HID, [(i, (i + k) % n_hid) for i in range(n_hid)])  23.5 us
    all_gather x1, waiting for transfers between devices, local(): lax.all_gather(lax.all_gather(jnp.concatenate([w_query, w_key, value_matr...  16.5 us
    unnamed x18, local copies, waits for them, and re-layouts  10.6 us
    dot_general x1, matrix products, local(): jnp.dot(heads_out, w_out, preferred_element_type=jnp.float32)  8.63 us
  transfers between devices with their start and end apart: 12, of which 9 were waited for; matrix products, arithmetic and copies ran while one was open for 13% of the time, Pallas kernels for 0%

commit v1 on v0

--- a/solution.py
+++ b/solution.py
@@ -62,8 +62,16 @@
     width_query = w_query.shape[1]
     width_kv = w_key.shape[1]
     stacked = lax.all_gather(
-        lax.all_gather(
-            jnp.concatenate([w_query, w_key, value_matrix], axis=1), "tz", axis=0, tiled=True
+        jnp.concatenate(
+            lax.all_to_all(
+                jnp.stack(
+                    [jnp.concatenate([w_query, w_key, value_matrix], axis=1)] * lax.axis_size("tz")
+                ),
+                "tz",
+                0,
+                0,
+            ),
+            axis=0,
         ),
         "tx",
         axis=0,

time: 283 us -> 307 us (1.085)
  blocking collectives: 0 us -> 73.7 us
  waiting for transfers between devices: 168 us -> 119 us
    all_to_all x0 -> x1, blocking collectives: none -> 73.7 us  [local(): lax.all_to_all(jnp.stack([jnp.concatenate([w_query, w_key, value_matrix],...]
    all_gather x2 -> x1, waiting for transfers between devices: 62.8 us -> 14.1 us  [local(): lax.all_gather(jnp.concatenate(lax.all_to_all(jnp.stack([jnp.concatenate(...]
    unnamed x18 -> x20, local copies, waits for them, and re-layouts: 10.6 us -> 9.49 us
  transfers between devices with their start and end apart: 12 -> 11, of which waited for: 9 -> 8; matrix products, arithmetic and copies ran while one was open for 13% -> 12% of each run, Pallas kernels for 0% -> 0%
where the time goes in v1:
time: 307 us; the launch traced here: 306 us
  waiting for transfers between devices  119 us (39%)
  blocking collectives  73.7 us (24%)
  matrix products  34.8 us (11%)
  starting transfers between devices  32.3 us (11%)
  local copies, waits for them, and re-layouts  17.5 us (6%)
  other arithmetic  15.2 us (5%)
  between operations  13.7 us (4%)
    all_to_all x1, blocking collectives, local(): lax.all_to_all(jnp.stack([jnp.concatenate([w_query, w_key, value_matrix],...  73.7 us
    reduce_scatter x1, waiting for transfers between devices, local(): lax.psum_scatter(partial_value.astype(jnp.bfloat16), HID, scatter_dimensi...  42.5 us
    ppermute x7, waiting for transfers between devices, local(): lax.ppermute(with_gain, HID, [(i, (i + k) % n_hid) for i in range(n_hid)])  35.8 us
    ppermute x2, waiting for transfers between devices, shifted(): lax.ppermute(value, axis, [(source, source + steps) for source in range(l...  26.6 us
    ppermute x7, starting transfers between devices, local(): lax.ppermute(with_gain, HID, [(i, (i + k) % n_hid) for i in range(n_hid)])  24.1 us
    all_gather x1, waiting for transfers between devices, local(): lax.all_gather(jnp.concatenate(lax.all_to_all(jnp.stack([jnp.concatenate(...  14.1 us
    unnamed x20, local copies, waits for them, and re-layouts  9.49 us
    dot_general x1, matrix products, local(): jnp.dot(heads_out, w_out, preferred_element_type=jnp.float32)  8.64 us
  transfers between devices with their start and end apart: 11, of which 8 were waited for; matrix products, arithmetic and copies ran while one was open for 12% of the time, Pallas kernels for 0%

profile of v1, /device:TPU:2, one launch (start us, length us, event | category | flops | bytes accessed | tf_op | source)
XLA Modules:
  0.0 306.2 jit_solution(8983438921325019421)
XLA Ops:
  6.5 0.0 all-gather.2.cloned.1.call-start
  6.5 1.1 pad_maximum_fusion.3
  7.7 0.0 copy-start.3
  7.7 0.3 stack.47
  8.0 0.0 copy-start.4
  8.0 0.0 copy-start.5
  8.0 73.7 %all_to_all.5 = bf16[8,168,1024]{2,1,0:T(8,128)(2,1)} all-to-all(bf16[8,168,1024]{2,1,0:T(8,128)(2,1)S(1)} %stack.47), channel_id=1, replica_groups=mesh['tx'=4,'tz'=8,'hy'=4,'hc'=2] {'tz'}, dimensions={0} | all-to-all | bytes 5505024 | tf_op jit(solution)/shard_map/all_to_all | solution.py:66
  81.8 0.0 all-gather.2.cloned.1.call-update
  81.8 0.0 reduce-scatter.2.cloned.1.call-start
  81.9 0.0 copy-done.2
  81.9 0.3 copy.19
  82.1 0.0 copy-done.3
  82.2 0.1 pad_maximum_fusion
  82.2 0.0 collective-permute-start
  82.3 1.7 collective-permute-start.1
  83.9 2.2 collective-permute-start.2
  86.1 1.8 collective-permute-start.3
  88.0 1.8 collective-permute-start.4
  89.9 0.5 multiply_cosine_fusion
  90.4 1.9 and_and_fusion
  92.3 0.0 copy-done.4
  92.3 0.0 copy-done.5
  92.4 1.0 bitcast_dynamic-update-slice_fusion.7
  93.3 9.7 %collective-permute-done = bf16[513,672]{1,0:T(8,128)(2,1)} collective-permute-done((bf16[513,672]{1,0:T(8,128)(2,1)S(1)}, bf16[513,672]{1,0:T(8,128)(2,1)}, u32[]{:S(2)}, u32[]{:S(2)}) %collective-permute-start) | collective-permute-done | bytes 689504 | tf_op jit(solution)/shard_map/ppermute | solution.py:52
  103.0 1.8 collective-permute-start.5
  104.8 2.1 bitcast_dynamic-update-slice_fusion.6
  106.9 0.0 collective-permute-done.1
  106.9 14.7 %collective-permute-start.6 = (bf16[513,672]{1,0:T(8,128)(2,1)S(1)}, bf16[513,672]{1,0:T(8,128)(2,1)S(1)}, u32[]{:S(2)}, u32[]{:S(2)}) collective-permute-start(bf16[513,672]{1,0:T(8,128)(2,1)S(1)} %pad_maximum_fusion), channel_id=1, source_target_pairs={{0,7},{1,0},{2,1},{3,2},{4,3},{5,4},{6,5},{7,6},{8,15},{9,8},{10,9... | collective-permute-start | bytes 2068424 | tf_op jit(solution)/shard_map/ppermute | solution.py:52
  121.6 2.1 bitcast_dynamic-update-slice_fusion.5
  123.8 14.7 %collective-permute-done.2 = bf16[513,672]{1,0:T(8,128)(2,1)} collective-permute-done((bf16[513,672]{1,0:T(8,128)(2,1)S(1)}, bf16[513,672]{1,0:T(8,128)(2,1)}, u32[]{:S(2)}, u32[]{:S(2)}) %collective-permute-start.2) | collective-permute-done | bytes 689504 | tf_op jit(solution)/shard_map/ppermute | solution.py:52
  138.5 2.1 bitcast_dynamic-update-slice_fusion.4
  140.5 0.0 collective-permute-done.3
  140.5 0.9 bitcast_dynamic-update-slice_fusion.3
  141.5 11.3 %collective-permute-done.4 = bf16[513,672]{1,0:T(8,128)(2,1)S(1)} collective-permute-done((bf16[513,672]{1,0:T(8,128)(2,1)S(1)}, bf16[513,672]{1,0:T(8,128)(2,1)S(1)}, u32[]{:S(2)}, u32[]{:S(2)}) %collective-permute-start.4) | collective-permute-done | bytes 689504 | tf_op jit(solution)/shard_map/ppermute | solution.py:52
  152.8 0.9 bitcast_dynamic-update-slice_fusion.2
  153.8 0.0 collective-permute-done.5
  153.8 1.0 bitcast_dynamic-update-slice_fusion.1
  154.8 0.1 collective-permute-done.6
  154.8 0.9 bitcast_dynamic-update-slice_fusion
  155.8 6.6 %gather_fusion = bf16[8,513,672]{2,1,0:T(8,128)(2,1)} fusion(bf16[8,513,672]{2,1,0:T(8,128)(2,1)} %bitcast_dynamic-update-slice_fusion, s32[1024]{0:T(1024)S(1)} %pad_clamp_fusion), kind=kCustom, calls=%fused_computation | custom fusion | bytes 11031584 | tf_op jit(solution)/shard_map/jit(_take)/gather | solution.py:56
  162.3 3.5 %broadcast_select_fusion = bf16[8,513,672]{2,1,0:T(8,128)(2,1)S(1)} fusion(bf16[8,513,672]{2,1,0:T(8,128)(2,1)} %gather_fusion, pred[8]{0:T(512)(128)(4,1)S(1)} %compare_and_fusion), kind=kLoop, calls=%fused_computation.11 | loop fusion | flops 2757888 | bytes 11031560 | tf_op jit(solution)/shard_map/jit(_take)/select_n | solution.py:56
  165.9 1.4 fusion.1
  167.3 4.7 %fusion.3 = bf16[8,512,672]{2,1,0:T(8,128)(2,1)} fusion(f32[8,672]{1,0:T(8,128)S(1)} %bitcast.87, f32[512]{0:T(512)S(1)} %add_rsqrt_fusion.2, bf16[8,513,672]{2,1,0:T(8,128)(2,1)S(1)} %broadcast_select_fusion), kind=kLoop, calls=%fused_computation.6 | loop fusion | flops 11010048 | bytes 11033600 | tf_op jit(solution)/shard_map/convert_element_type | solution.py:61
  171.9 14.1 %all-gather.2.cloned.1.call-done = bf16[5376,1024]{1,0:T(8,128)(2,1)} async-done(((bf16[1344,1024]{1,0:T(8,128)(2,1)}), bf16[5376,1024]{1,0:T(8,128)(2,1)}) %all-gather.2.cloned.1.call-update) | async-done | bytes 11010064 | tf_op jit(solution)/shard_map/all_gather | solution.py:64
  186.1 8.3 %fusion.14 = f32[512,512]{0,1:T(8,128)S(1)} fusion(bf16[8,512,672]{2,1,0:T(8,128)(2,1)} %fusion.3, bf16[8,672,1024]{2,1,0:T(8,128)(2,1)} %bitcast.88), kind=kOutput, calls=%fused_computation.23 | convolution fusion | flops 2818572288 | bytes 12845056 | tf_op jit(solution)/shard_map/jrc,jcn->rn/dot_general | solution.py:81
  194.4 0.1 multiply_reduce_fusion.1
  194.5 0.1 multiply_multiply_fusion.1
  194.6 0.1 subtract_convert_fusion.1
  194.8 4.5 %collective-permute-start.7 = (bf16[512,512]{0,1:T(8,128)(2,1)S(1)}, bf16[512,512]{0,1:T(8,128)(2,1)S(1)}, u32[]{:S(2)}, u32[]{:S(2)}) collective-permute-start(bf16[512,512]{0,1:T(8,128)(2,1)S(1)} %pad_maximum_fusion.1), channel_id=1, source_target_pairs={{0,16},{8,24},{16,32},{24,40},{32,48},{40,56},{48,64},{56,72},{64,... | collective-permute-start | bytes 1572872 | tf_op jit(solution)/shard_map/ppermute | solution.py:17
  199.3 3.7 %collective-permute-start.8 = (bf16[512,512]{0,1:T(8,128)(2,1)S(1)}, bf16[512,512]{0,1:T(8,128)(2,1)S(1)}, u32[]{:S(2)}, u32[]{:S(2)}) collective-permute-start(bf16[512,512]{0,1:T(8,128)(2,1)S(1)} %pad_maximum_fusion.1), channel_id=1, source_target_pairs={{0,8},{8,16},{16,24},{24,32},{32,40},{40,48},{48,56},{56,64},{64,7... | collective-permute-start | bytes 1572872 | tf_op jit(solution)/shard_map/ppermute | solution.py:17
  203.0 0.0 copy-done
  203.0 5.5 %fusion.10 = f32[512,512,1]{0,1,2:T(8,128)S(1)} fusion(bf16[8,512,672]{2,1,0:T(8,128)(2,1)S(1)} %copy-done, bf16[8,672,1024]{2,1,0:T(8,128)(2,1)} %bitcast.89), kind=kOutput, calls=%fused_computation.17 | convolution fusion | flops 2818572288 | bytes 12058624 | tf_op jit(solution)/shard_map/jrc,jcn->rn/dot_general | solution.py:94
  208.5 0.1 multiply_reduce_fusion
  208.7 0.2 multiply_multiply_fusion
  208.9 0.2 subtract_convert_fusion
  209.1 15.8 %collective-permute-done.7 = bf16[512,512]{0,1:T(8,128)(2,1)S(1)} collective-permute-done((bf16[512,512]{0,1:T(8,128)(2,1)S(1)}, bf16[512,512]{0,1:T(8,128)(2,1)S(1)}, u32[]{:S(2)}, u32[]{:S(2)}) %collective-permute-start.7) | collective-permute-done | bytes 524320 | tf_op jit(solution)/shard_map/ppermute | solution.py:17
  224.9 10.8 %collective-permute-done.8 = bf16[512,512]{0,1:T(8,128)(2,1)S(1)} collective-permute-done((bf16[512,512]{0,1:T(8,128)(2,1)S(1)}, bf16[512,512]{0,1:T(8,128)(2,1)S(1)}, u32[]{:S(2)}, u32[]{:S(2)}) %collective-permute-start.8) | collective-permute-done | bytes 524320 | tf_op jit(solution)/shard_map/ppermute | solution.py:17
  235.7 0.1 maximum_maximum_fusion
  235.8 0.1 fusion.35
  235.9 8.5 %fusion.36 = (f32[2,2,512]{2,1,0:T(2,128)S(1)}, bf16[2,2,512,1536]{2,3,1,0:T(8,128)(2,1)}) fusion(pred[512,1536]{0,1:T(8,128)(4,1)S(1)} %copy-done.1, bf16[1536,2,128,1]{0,2,3,1:T(8,128)(2,1)S(1)} %bitcast.85, bf16[512,2,2,128]{0,3,2,1:T(8,128)(2,1)S(1)} %bitcast.86), kind=kOutput, calls=%fused_computation.81 | convolution fusion | flops 824182272 | bytes 8396800 | tf_op jit(solution)/shard_map/sub | solution.py:119
  244.4 3.8 %fusion.25 = bf16[512,2,2,128]{0,3,2,1:T(8,128)(2,1)S(1)} fusion(bf16[1536,2,128,1]{0,2,3,1:T(8,128)(2,1)S(1)} %bitcast.84, bf16[2,2,512,1536]{2,3,1,0:T(8,128)(2,1)} %get-tuple-element.16, f32[512,2,2]{0,2,1:T(2,128)S(1)} %bitcast.91), kind=kOutput, calls=%fused_computation.27 | convolution fusion | flops 805830656 | bytes 7610368 | tf_op jit(solution)/shard_map/kgts,skd->tkgd/dot_general | solution.py:122
  248.2 8.6 %convolution_convert_fusion = bf16[512,5376]{0,1:T(8,128)(2,1)} fusion(bf16[512,512]{0,1:T(8,128)(2,1)S(1)} %bitcast.90, bf16[512,5376]{1,0:T(8,128)(2,1)} %param.15), kind=kOutput, calls=%fused_computation.10 | convolution fusion | flops 2821324800 | bytes 11534336 | tf_op jit(solution)/shard_map/dot_general | solution.py:127
  256.8 0.0 reduce-scatter.2.cloned.1.call-update
  256.8 42.5 %reduce-scatter.2.cloned.1.call-done = bf16[512,672]{0,1:T(8,128)(2,1)} async-done(((bf16[512,5376]{0,1:T(8,128)(2,1)}), bf16[512,672]{0,1:T(8,128)(2,1)}) %reduce-scatter.2.cloned.1.call-update) | async-done | bytes 688144 | tf_op jit(solution)/shard_map/reduce_scatter | solution.py:128
  (23 shorter events, 0.3 us)
Async XLA Ops:
  6.5 75.3 %copy-start.2 = (bf16[512,672]{0,1:T(8,128)(2,1)S(1)}, bf16[512,672]{0,1:T(8,128)(2,1)}, u32[]{:S(2)}) copy-start(bf16[512,672]{0,1:T(8,128)(2,1)} %param.8) | copy-start | bytes 2064388
  6.5 179.5 %all-gather.2.cloned.1.call-start = ((), (), s32[]{:S(2)}) async-start(), calls=%async_computation.2 | async-start | bytes 13762560 | tf_op jit(solution)/shard_map/all_gather | solution.py:64
  7.7 74.5 %copy-start.3 = (bf16[1,672]{1,0:T(2,128)(2,1)S(1)}, bf16[1,672]{1,0:T(2,128)(2,1)}, u32[]{:S(2)}) copy-start(bf16[1,672]{1,0:T(2,128)(2,1)} %param.9) | copy-start | bytes 4036
  8.0 84.3 %copy-start.4 = (bf16[1,128]{1,0:T(2,128)(2,1)S(1)}, bf16[1,128]{1,0:T(2,128)(2,1)}, u32[]{:S(2)}) copy-start(bf16[1,128]{1,0:T(2,128)(2,1)} %param.14) | copy-start | bytes 772
  8.0 84.3 %copy-start.5 = (bf16[1,128]{1,0:T(2,128)(2,1)S(1)}, bf16[1,128]{1,0:T(2,128)(2,1)}, u32[]{:S(2)}) copy-start(bf16[1,128]{1,0:T(2,128)(2,1)} %param.13) | copy-start | bytes 772
  81.8 217.6 %reduce-scatter.2.cloned.1.call-start = ((), (), s32[]{:S(2)}) async-start(), calls=%async_computation.3 | async-start | bytes 6193152 | tf_op jit(solution)/shard_map/reduce_scatter | solution.py:128
  82.2 20.8 %collective-permute-start = (bf16[513,672]{1,0:T(8,128)(2,1)S(1)}, bf16[513,672]{1,0:T(8,128)(2,1)}, u32[]{:S(2)}, u32[]{:S(2)}) collective-permute-start(bf16[513,672]{1,0:T(8,128)(2,1)S(1)} %pad_maximum_fusion), channel_id=1, source_target_pairs={{0,1},{1,2},{2,3},{3,4},{4,5},{5,6},{6,7},{7,0},{8,9},{9,10},{10,1... | collective-permute-start | bytes 2068424 | tf_op jit(solution)/shard_map/ppermute | solution.py:52
  82.3 24.6 %collective-permute-start.1 = (bf16[513,672]{1,0:T(8,128)(2,1)S(1)}, bf16[513,672]{1,0:T(8,128)(2,1)}, u32[]{:S(2)}, u32[]{:S(2)}) collective-permute-start(bf16[513,672]{1,0:T(8,128)(2,1)S(1)} %pad_maximum_fusion), channel_id=1, source_target_pairs={{0,2},{1,3},{2,4},{3,5},{4,6},{5,7},{6,0},{7,1},{8,10},{9,11},{10,... | collective-permute-start | bytes 2068424 | tf_op jit(solution)/shard_map/ppermute | solution.py:52
  83.9 54.6 %collective-permute-start.2 = (bf16[513,672]{1,0:T(8,128)(2,1)S(1)}, bf16[513,672]{1,0:T(8,128)(2,1)}, u32[]{:S(2)}, u32[]{:S(2)}) collective-permute-start(bf16[513,672]{1,0:T(8,128)(2,1)S(1)} %pad_maximum_fusion), channel_id=1, source_target_pairs={{0,3},{1,4},{2,5},{3,6},{4,7},{5,0},{6,1},{7,2},{8,11},{9,12},{10,... | collective-permute-start | bytes 2068424 | tf_op jit(solution)/shard_map/ppermute | solution.py:52
  86.1 54.4 %collective-permute-start.3 = (bf16[513,672]{1,0:T(8,128)(2,1)S(1)}, bf16[513,672]{1,0:T(8,128)(2,1)S(1)}, u32[]{:S(2)}, u32[]{:S(2)}) collective-permute-start(bf16[513,672]{1,0:T(8,128)(2,1)S(1)} %pad_maximum_fusion), channel_id=1, source_target_pairs={{0,4},{1,5},{2,6},{3,7},{4,0},{5,1},{6,2},{7,3},{8,12},{9,13},{10,... | collective-permute-start | bytes 2068424 | tf_op jit(solution)/shard_map/ppermute | solution.py:52
  88.0 64.9 %collective-permute-start.4 = (bf16[513,672]{1,0:T(8,128)(2,1)S(1)}, bf16[513,672]{1,0:T(8,128)(2,1)S(1)}, u32[]{:S(2)}, u32[]{:S(2)}) collective-permute-start(bf16[513,672]{1,0:T(8,128)(2,1)S(1)} %pad_maximum_fusion), channel_id=1, source_target_pairs={{0,5},{1,6},{2,7},{3,0},{4,1},{5,2},{6,3},{7,4},{8,13},{9,14},{10,... | collective-permute-start | bytes 2068424 | tf_op jit(solution)/shard_map/ppermute | solution.py:52
  103.0 50.8 %collective-permute-start.5 = (bf16[513,672]{1,0:T(8,128)(2,1)S(1)}, bf16[513,672]{1,0:T(8,128)(2,1)S(1)}, u32[]{:S(2)}, u32[]{:S(2)}) collective-permute-start(bf16[513,672]{1,0:T(8,128)(2,1)S(1)} %pad_maximum_fusion), channel_id=1, source_target_pairs={{0,6},{1,7},{2,0},{3,1},{4,2},{5,3},{6,4},{7,5},{8,14},{9,15},{10,... | collective-permute-start | bytes 2068424 | tf_op jit(solution)/shard_map/ppermute | solution.py:52
  106.9 47.9 %collective-permute-start.6 = (bf16[513,672]{1,0:T(8,128)(2,1)S(1)}, bf16[513,672]{1,0:T(8,128)(2,1)S(1)}, u32[]{:S(2)}, u32[]{:S(2)}) collective-permute-start(bf16[513,672]{1,0:T(8,128)(2,1)S(1)} %pad_maximum_fusion), channel_id=1, source_target_pairs={{0,7},{1,0},{2,1},{3,2},{4,3},{5,4},{6,5},{7,6},{8,15},{9,8},{10,9... | collective-permute-start | bytes 2068424 | tf_op jit(solution)/shard_map/ppermute | solution.py:52
  186.1 16.9 %copy-start = (bf16[8,512,672]{2,1,0:T(8,128)(2,1)S(1)}, bf16[8,512,672]{2,1,0:T(8,128)(2,1)}, u32[]{:S(2)}) copy-start(bf16[8,512,672]{2,1,0:T(8,128)(2,1)} %fusion.3) | copy-start | bytes 16515076
  194.8 30.0 %collective-permute-start.7 = (bf16[512,512]{0,1:T(8,128)(2,1)S(1)}, bf16[512,512]{0,1:T(8,128)(2,1)S(1)}, u32[]{:S(2)}, u32[]{:S(2)}) collective-permute-start(bf16[512,512]{0,1:T(8,128)(2,1)S(1)} %pad_maximum_fusion.1), channel_id=1, source_target_pairs={{0,16},{8,24},{16,32},{24,40},{32,48},{40,56},{48,64},{56,72},{64,... | collective-permute-start | bytes 1572872 | tf_op jit(solution)/shard_map/ppermute | solution.py:17
  199.3 36.4 %collective-permute-start.8 = (bf16[512,512]{0,1:T(8,128)(2,1)S(1)}, bf16[512,512]{0,1:T(8,128)(2,1)S(1)}, u32[]{:S(2)}, u32[]{:S(2)}) collective-permute-start(bf16[512,512]{0,1:T(8,128)(2,1)S(1)} %pad_maximum_fusion.1), channel_id=1, source_target_pairs={{0,8},{8,16},{16,24},{24,32},{32,40},{40,48},{48,56},{56,64},{64,7... | collective-permute-start | bytes 1572872 | tf_op jit(solution)/shard_map/ppermute | solution.py:17
  208.5 27.4 %copy-start.1 = (pred[512,1536]{0,1:T(8,128)(4,1)S(1)}, pred[512,1536]{0,1:T(8,128)(4,1)}, u32[]{:S(2)}) copy-start(pred[512,1536]{0,1:T(8,128)(4,1)} %and_and_fusion) | copy-start | bytes 2359300
Sparse Core Ops, SparseCore 0:
  81.9 104.0 all-gather.1
  257.0 42.3 reduce-scatter.1
